TPU v7x, 32 devices: a whole 2x2x4 slice. The times are simulated.
32 devices in a mesh: tm: 16 (over z, y, x), sec: 2 (over core).
Axes of the slice: x: 2, y: 2, z: 4, core: 2. Of those that a mesh axis runs over, the one named last changes fastest.
Arguments:
- signal: bfloat16 [2048, 16384], P('sec', 'tm')
- round_shard: int32 [2], replicated, may hold values from 0 to 15
- offsets: int32 [2, 16], replicated, may hold values from 0 to 896
- chan_range: int32 [2, 16, 2], replicated, may hold values from 0 to 2048, as said below
Outputs:
- detection: float32 [2, 16, 16384], P(None, None, 'tm')
Inputs may be any that keep to these rules, and one draw needn't show every extreme that they name: chan_range[r, k] = (lo, hi) with lo < hi and hi - lo >= 512.
All inputs are finite; a program needn't handle non-finite values.
Results may differ from a plain program's by a relative error of at most 0.0003.
Values may be sent and summed in bfloat16 or wider, within the bound.
No kernel may reach another device: no remote copies, remote signals or barrier semaphores. Data moves between devices by JAX's collectives and lax.ppermute only.
A program may use at most 64 MiB of HBM per device.

v0:
```python
import jax
import jax.numpy as jnp
from jax import lax
from jax.sharding import PartitionSpec as P

L = 128
TPL_BLOCK = 4
ROUNDS = 2
EPS = 1e-06


def from_behind(value, axis, by):
    length = lax.axis_size(axis)
    pairs = [(i, i + by) for i in range(length) if 0 <= i + by < length]
    return lax.ppermute(value, axis, pairs)


def spread(value, axis, source):
    kept = jnp.where(lax.axis_index(axis) == source, value, 0).astype(value.dtype)
    return lax.psum(kept, axis)


def skew_sum(product, lag_count):
    group_count, tap_count, span_width = product.shape
    flipped = product[:, :, ::-1]
    widened = jnp.pad(flipped, ((0, 0), (0, 0), (0, 1)))
    sheared = widened.reshape(group_count, tap_count * (span_width + 1))[
        :, : tap_count * span_width
    ]
    sheared = sheared.reshape(group_count, tap_count, span_width)
    summed = jnp.sum(sheared, axis=1)
    return summed[:, span_width - lag_count :][:, ::-1]


def correlate(templates, extended, lag_count):
    template_count = templates.shape[0]
    grouped = templates.reshape(
        template_count // TPL_BLOCK, TPL_BLOCK, templates.shape[1], templates.shape[2]
    )

    def one_block(block):
        product = jnp.einsum("kcl,cw->klw", block, extended, preferred_element_type=jnp.float32)
        return skew_sum(product, lag_count)

    return lax.map(one_block, grouped).reshape(template_count, lag_count)


def sliding_energy(masks, extended, lag_count, tap_count):
    squares = jnp.square(extended.astype(jnp.float32))
    summed = jnp.dot(
        masks, squares, precision=lax.Precision.HIGHEST, preferred_element_type=jnp.float32
    )
    running = jnp.pad(jnp.cumsum(summed, axis=1), ((0, 0), (1, 0)))
    return running[:, tap_count : tap_count + lag_count] - running[:, :lag_count]


def cut_windows(records, starts, inside):
    windows = jax.vmap(lambda first: lax.dynamic_slice_in_dim(records, first, L, axis=1))(starts)
    return jnp.where(inside[:, :, None], windows, jnp.zeros_like(windows))


def shards(signal, round_shard, offsets, chan_range):
    chan_local = signal.shape[0]
    lag_count = signal.shape[1]
    section = lax.axis_index("sec")
    total_lags = lag_count * lax.axis_size("tm")
    right_rim = from_behind(signal[:, :L], "tm", -1)
    extended = jnp.concatenate([signal, right_rim], axis=1)
    channel = section * chan_local + jnp.arange(chan_local, dtype=jnp.int32)

    def make_template(level):
        lower = chan_range[level, :, 0]
        upper = chan_range[level, :, 1]
        inside = (channel[None, :] >= lower[:, None]) & (channel[None, :] < upper[:, None])
        local_tmpl = cut_windows(signal, offsets[level], inside)
        templates = spread(local_tmpl, "tm", round_shard[level])
        local_power = jnp.sum(jnp.square(templates.astype(jnp.float32)), axis=(1, 2))
        tmpl_power = lax.psum(local_power, "sec")
        return (templates, inside.astype(jnp.float32), tmpl_power)

    def finish(templates, masks, tmpl_power):
        corr_local = correlate(templates, extended, lag_count)
        energy_local = sliding_energy(masks, extended, lag_count, L)
        corr, energy = lax.psum((corr_local, energy_local), "sec")
        normed = corr / jnp.sqrt(energy * tmpl_power[:, None] + EPS)
        power_sum = lax.psum(jnp.sum(normed * normed, axis=1), "tm")
        meansq = power_sum / total_lags
        scored = normed / jnp.sqrt(meansq[:, None] + EPS)
        return scored

    results = [finish(*make_template(level)) for level in range(ROUNDS)]
    return jnp.stack(results, axis=0)


def solution(mesh):
    placed = (P("sec", "tm"), P(), P(), P())
    return jax.shard_map(
        shards, mesh=mesh, in_specs=placed, out_specs=P(None, None, "tm"), check_vma=False
    )
```

profile of v0, /device:TPU:0, one launch (start us, length us, event | category | flops | bytes accessed | tf_op | source)
XLA Modules:
  0.0 749.8 jit_solution(7222854212829165390)
XLA Ops:
  10.8 2.7 broadcast.163.clone.1
  13.5 49.9 %while.28 = (s32[]{:T(128)}, bf16[1024,1024]{1,0:T(8,128)(2,1)}, s32[16,2]{0,1:T(2,128)S(1)}, bf16[16,1024,128]{2,1,0:T(8,128)(2,1)}, s32[]{:T(128)}) while((s32[]{:T(128)}, bf16[1024,1024]{1,0:T(8,128)(2,1)}, s32[16,2]{0,1:T(2,128)S(1)}, bf16[16,1024,128]{2,1,0:T(8,128)(2,1)}, s32[]{:T(128)}) %tuple.84), condition=%wide.while_cond, body=%wide.while_body.sunk | while | flops 2 | bytes 525401 | solution.py:58
  63.4 2.8 broadcast.163.clone
  66.2 49.9 %while.29 = (s32[]{:T(128)}, bf16[1024,1024]{1,0:T(8,128)(2,1)}, s32[16,2]{0,1:T(2,128)S(1)}, bf16[16,1024,128]{2,1,0:T(8,128)(2,1)}, s32[]{:T(128)}) while((s32[]{:T(128)}, bf16[1024,1024]{1,0:T(8,128)(2,1)}, s32[16,2]{0,1:T(2,128)S(1)}, bf16[16,1024,128]{2,1,0:T(8,128)(2,1)}, s32[]{:T(128)}) %tuple.102), condition=%wide.while_cond.1, body=%wide.while_body.1.sunk | while | flops 2 | bytes 525401 | solution.py:58
  76.1 2.5 bitcast_dynamic-update-slice_fusion.11
  116.2 8.0 %select_select_fusion = (bf16[16,1024,128]{2,1,0:T(8,128)(2,1)}, bf16[16,1024,128]{2,1,0:T(8,128)(2,1)}) fusion(bf16[16,1024,128]{2,1,0:T(8,128)(2,1)} %get-tuple-element.128, pred[16,1024]{1,0:T(8,128)(4,1)S(1)} %get-tuple-element.188, pred[]{:T(512)S(6)} %eq.7, bf16[16,1024,128]{2,1,0:T(8,128)(2,1)} %get-tuple-element.120, ...), kind=kLoop, calls=%fused_computation.23 | loop fusion | flops 8388608 | bytes 16809986 | tf_op jit(solution)/shard_map/jit(_where)/select_n | solution.py:19
  128.3 10.6 %collective-permute-done = bf16[1024,128]{1,0:T(8,128)(2,1)S(1)} collective-permute-done((bf16[1024,128]{1,0:T(8,128)(2,1)S(1)}, bf16[1024,128]{1,0:T(8,128)(2,1)S(1)}, u32[]{:S(2)}, u32[]{:S(2)}) %collective-permute-start) | collective-permute-done | bytes 262176 | tf_op jit(solution)/shard_map/ppermute | solution.py:15
  141.0 4.7 reduce-window.16
  148.1 4.5 reduce-window.14
  153.9 233.3 %all-reduce.15.cloned.1.call-done = (bf16[16,1024,128]{2,1,0:T(8,128)(2,1)}, bf16[16,1024,128]{2,1,0:T(8,128)(2,1)}) async-done(((bf16[16,1024,128]{2,1,0:T(8,128)(2,1)}, bf16[16,1024,128]{2,1,0:T(8,128)(2,1)}), (bf16[16,1024,128]{2,1,0:T(8,128)(2,1)}, bf16[16,1024,128]{2,1,0:T(8,128)(2,1)})) %all-reduce.15.cloned.1.call-update) | async-done | bytes 8388624 | tf_op jit(solution)/shard_map/psum | solution.py:20
  387.3 3.2 multiply_reduce_fusion
  390.4 143.4 %while.26 = (s32[]{:T(128)}, f32[4,4,1024]{2,1,0:T(4,128)S(1)}, bf16[4,4,1024,128]{3,2,1,0:T(8,128)(2,1)}, bf16[1024,1152]{1,0:T(8,128)(2,1)S(1)}, s32[]{:T(128)}, /*index=5*/f32[]{:T(128)}) while((s32[]{:T(128)}, f32[4,4,1024]{2,1,0:T(4,128)S(1)}, bf16[4,4,1024,128]{3,2,1,0:T(8,128)(2,1)}, bf16[1024,1152]{1,0:T(8,128)(2,1)S(1)}, s32[]{:T(128)}, ...), condition=%wide.region_3.4_spmd, body=%wide.region_1.3_spmd.sunk | while | flops 1208544768 | bytes 29483620 | solution.py:45
  390.5 4.3 fusion.23
  394.7 19.8 %rev.28 = f32[4,128,1152]{2,1,0:T(8,128)} reverse(f32[4,128,1152]{2,1,0:T(8,128)} %fusion.23), dimensions={2} | reverse | bytes 4718592 | tf_op jit(solution)/shard_map/while/body/eval_jaxpr/rev | solution.py:25
  414.5 3.5 pad.40
  418.0 5.8 reshape.302
  426.3 4.3 fusion.23
  430.6 19.8 %rev.28 = f32[4,128,1152]{2,1,0:T(8,128)} reverse(f32[4,128,1152]{2,1,0:T(8,128)} %fusion.23), dimensions={2} | reverse | bytes 4718592 | tf_op jit(solution)/shard_map/while/body/eval_jaxpr/rev | solution.py:25
  450.3 3.5 pad.40
  453.8 5.8 reshape.302
  462.2 4.3 fusion.23
  466.4 19.8 %rev.28 = f32[4,128,1152]{2,1,0:T(8,128)} reverse(f32[4,128,1152]{2,1,0:T(8,128)} %fusion.23), dimensions={2} | reverse | bytes 4718592 | tf_op jit(solution)/shard_map/while/body/eval_jaxpr/rev | solution.py:25
  486.2 3.5 pad.40
  489.6 5.8 reshape.302
  498.0 4.3 fusion.23
  502.3 19.8 %rev.28 = f32[4,128,1152]{2,1,0:T(8,128)} reverse(f32[4,128,1152]{2,1,0:T(8,128)} %fusion.23), dimensions={2} | reverse | bytes 4718592 | tf_op jit(solution)/shard_map/while/body/eval_jaxpr/rev | solution.py:25
  522.0 3.5 pad.40
  525.5 5.8 reshape.302
  534.5 143.4 %while.27 = (s32[]{:T(128)}, f32[4,4,1024]{2,1,0:T(4,128)S(1)}, bf16[4,4,1024,128]{3,2,1,0:T(8,128)(2,1)}, bf16[1024,1152]{1,0:T(8,128)(2,1)S(1)}, s32[]{:T(128)}, /*index=5*/f32[]{:T(128)}) while((s32[]{:T(128)}, f32[4,4,1024]{2,1,0:T(4,128)S(1)}, bf16[4,4,1024,128]{3,2,1,0:T(8,128)(2,1)}, bf16[1024,1152]{1,0:T(8,128)(2,1)S(1)}, ...), condition=%wide.region_15.16_spmd, body=%wide.region_13.15_spmd.sunk | while | flops 1208544768 | bytes 29483620 | solution.py:45
  534.5 4.3 fusion.26
  538.8 19.8 %rev.30 = f32[4,128,1152]{2,1,0:T(8,128)} reverse(f32[4,128,1152]{2,1,0:T(8,128)} %fusion.26), dimensions={2} | reverse | bytes 4718592 | tf_op jit(solution)/shard_map/while/body/eval_jaxpr/rev | solution.py:25
  558.6 3.5 pad.41
  562.0 5.8 reshape.303
  570.4 4.3 fusion.26
  574.6 19.8 %rev.30 = f32[4,128,1152]{2,1,0:T(8,128)} reverse(f32[4,128,1152]{2,1,0:T(8,128)} %fusion.26), dimensions={2} | reverse | bytes 4718592 | tf_op jit(solution)/shard_map/while/body/eval_jaxpr/rev | solution.py:25
  594.4 3.5 pad.41
  597.9 5.8 reshape.303
  606.2 4.3 fusion.26
  610.5 19.8 %rev.30 = f32[4,128,1152]{2,1,0:T(8,128)} reverse(f32[4,128,1152]{2,1,0:T(8,128)} %fusion.26), dimensions={2} | reverse | bytes 4718592 | tf_op jit(solution)/shard_map/while/body/eval_jaxpr/rev | solution.py:25
  630.2 3.5 pad.41
  633.7 5.8 reshape.303
  642.1 4.3 fusion.26
  646.3 19.8 %rev.30 = f32[4,128,1152]{2,1,0:T(8,128)} reverse(f32[4,128,1152]{2,1,0:T(8,128)} %fusion.26), dimensions={2} | reverse | bytes 4718592 | tf_op jit(solution)/shard_map/while/body/eval_jaxpr/rev | solution.py:25
  666.1 3.5 pad.41
  669.6 5.8 reshape.303
  678.6 3.2 multiply_reduce_fusion.1
  684.2 11.9 %all-reduce.13.cloned.1.call-done = (f32[16,1024]{1,0:T(8,128)}, f32[16,1024]{1,0:T(8,128)}, f32[16,1024]{1,0:T(8,128)}, f32[16,1024]{1,0:T(8,128)}) async-done(((f32[16,1024]{1,0:T(8,128)}, f32[16,1024]{1,0:T(8,128)}, f32[16,1024]{1,0:T(8,128)}, f32[16,1024]{1,0:T(8,128)}), (f32[16,1024]{1,0:T(8,128)}, f32[16,1024]{1,0:T(8,128)}, f32[16,1024]{1,0:T(8,128)}, ...) | async-done | bytes 262160 | tf_op jit(solution)/shard_map/psum | solution.py:84
  698.3 42.0 %all-reduce.6 = (f32[16]{0:T(128)S(1)}, f32[16]{0:T(128)S(1)}) all-reduce(f32[16]{0:T(128)S(1)} %multiply_reduce_fusion.2, f32[16]{0:T(128)S(1)} %multiply_reduce_fusion.3), channel_id=1, replica_groups=mesh['tm'=16,'sec'=2] {'tm'}, use_global_device_ids=true, to_apply=%region_23.24 | all-reduce | flops 32 | bytes 256 | tf_op jit(solution)/shard_map/psum | solution.py:86
  (183 shorter events, 138.9 us)
Async XLA Ops:
  6.5 380.7 %all-reduce.15.cloned.1.call-start = ((), (), s32[]{:S(2)}) async-start(), calls=%async_computation.1 | async-start | bytes 16777216 | tf_op jit(solution)/shard_map/psum | solution.py:20
  124.2 571.9 %all-reduce.13.cloned.1.call-start = ((), (), s32[]{:S(2)}) async-start(), calls=%async_computation | async-start | bytes 524288 | tf_op jit(solution)/shard_map/psum | solution.py:84
  125.3 13.7 %collective-permute-start = (bf16[1024,128]{1,0:T(8,128)(2,1)S(1)}, bf16[1024,128]{1,0:T(8,128)(2,1)S(1)}, u32[]{:S(2)}, u32[]{:S(2)}) collective-permute-start(bf16[1024,128]{1,0:T(8,128)(2,1)S(1)} %slice.81), channel_id=1, source_target_pairs={{2,0},{4,2},{6,4},{8,6},{10,8},{12,10},{14,12},{16,14},{18,16},{20... | collective-permute-start | bytes 786440 | tf_op jit(solution)/shard_map/ppermute | solution.py:15
  423.8 1.7 slice-start
  459.6 1.7 slice-start
  495.4 1.7 slice-start
  531.3 1.7 slice-start
  567.8 1.7 slice-start.1
  603.7 1.7 slice-start.1
  639.5 1.7 slice-start.1
  675.4 1.7 slice-start.1
Sparse Core Ops, SparseCore 0:
  124.4 262.8 all-reduce.14
  678.7 17.4 all-reduce.12
where the time goes:
time: 764 us; the launch traced here: 750 us
  local copies, waits for them, and re-layouts  364 us (48%)
  waiting for transfers between devices  256 us (34%)
  blocking collectives  44.4 us (6%)
  matrix products  37.8 us (5%)
  other arithmetic  31.7 us (4%)
  between operations  14.8 us (2%)
    psum x1, waiting for transfers between devices, spread(): return lax.psum(kept, axis)  233 us
    rev x8, local copies, waits for them, and re-layouts, skew_sum(): flipped = product[:, :, ::-1]  158 us
    gather x96, local copies, waits for them, and re-layouts  99.8 us
    reshape x8, local copies, waits for them, and re-layouts, skew_sum(): widened.reshape(group_count, tap_count * (span_width + 1))  46.4 us
    psum x1, blocking collectives, finish(): power_sum = lax.psum(jnp.sum(normed * normed, axis=1), 'tm')  42 us
    dot_general x8, matrix products, one_block(): jnp.einsum('kcl,cw->klw', block, extended, preferred_element_type=jnp.flo...  34 us
    pad x8, local copies, waits for them, and re-layouts, skew_sum(): widened = jnp.pad(flipped, ((0, 0), (0, 0), (0, 1)))  27.8 us
  transfers between devices with their start and end apart: 3, of which 3 were waited for; matrix products, arithmetic and copies ran while one was open for 3% of the time, Pallas kernels for 0%

commit v1 on v0

--- a/solution.py
+++ b/solution.py
@@ -83,7 +83,9 @@
         energy_local = sliding_energy(masks, extended, lag_count, L)
         corr, energy = lax.psum((corr_local, energy_local), "sec")
         normed = corr / jnp.sqrt(energy * tmpl_power[:, None] + EPS)
-        power_sum = lax.psum(jnp.sum(normed * normed, axis=1), "tm")
+        inputs = jnp.sum(normed * normed, axis=1)
+        z1 = lax.all_gather(inputs, "tm")
+        power_sum = jnp.sum(z1, axis=0)
         meansq = power_sum / total_lags
         scored = normed / jnp.sqrt(meansq[:, None] + EPS)
         return scored

time: 764 us -> 765 us (level)
    psum x1 -> x0, blocking collectives: 42 us -> none  [finish(): power_sum = lax.psum(jnp.sum(normed * normed, axis=1), 'tm')]
    unnamed x0 -> x1, blocking collectives: none -> 42 us
where the time goes in v1:
time: 765 us; the launch traced here: 750 us
  local copies, waits for them, and re-layouts  365 us (48%)
  waiting for transfers between devices  255 us (33%)
  blocking collectives  44.4 us (6%)
  matrix products  37.8 us (5%)
  other arithmetic  31.8 us (4%)
  between operations  15.4 us (2%)
    psum x1, waiting for transfers between devices, spread(): return lax.psum(kept, axis)  233 us
    rev x8, local copies, waits for them, and re-layouts, skew_sum(): flipped = product[:, :, ::-1]  158 us
    gather x96, local copies, waits for them, and re-layouts  99.8 us
    reshape x8, local copies, waits for them, and re-layouts, skew_sum(): widened.reshape(group_count, tap_count * (span_width + 1))  46.4 us
    unnamed x1, blocking collectives  42 us
    dot_general x8, matrix products, one_block(): jnp.einsum('kcl,cw->klw', block, extended, preferred_element_type=jnp.flo...  34 us
    pad x8, local copies, waits for them, and re-layouts, skew_sum(): widened = jnp.pad(flipped, ((0, 0), (0, 0), (0, 1)))  27.8 us
  transfers between devices with their start and end apart: 3, of which 3 were waited for; matrix products, arithmetic and copies ran while one was open for 3% of the time, Pallas kernels for 0%

profile of v1, /device:TPU:0, one launch (start us, length us, event | category | flops | bytes accessed | tf_op | source)
XLA Modules:
  0.0 750.5 jit_solution(8553308981506715061)
XLA Ops:
  10.8 2.7 broadcast.177.clone.1
  13.5 49.9 %while.28 = (s32[]{:T(128)}, bf16[1024,1024]{1,0:T(8,128)(2,1)}, s32[16,2]{0,1:T(2,128)S(1)}, bf16[16,1024,128]{2,1,0:T(8,128)(2,1)}, s32[]{:T(128)}) while((s32[]{:T(128)}, bf16[1024,1024]{1,0:T(8,128)(2,1)}, s32[16,2]{0,1:T(2,128)S(1)}, bf16[16,1024,128]{2,1,0:T(8,128)(2,1)}, s32[]{:T(128)}) %tuple.86), condition=%wide.while_cond, body=%wide.while_body.sunk | while | flops 2 | bytes 525401 | solution.py:58
  63.4 2.8 broadcast.177.clone
  66.2 49.9 %while.29 = (s32[]{:T(128)}, bf16[1024,1024]{1,0:T(8,128)(2,1)}, s32[16,2]{0,1:T(2,128)S(1)}, bf16[16,1024,128]{2,1,0:T(8,128)(2,1)}, s32[]{:T(128)}) while((s32[]{:T(128)}, bf16[1024,1024]{1,0:T(8,128)(2,1)}, s32[16,2]{0,1:T(2,128)S(1)}, bf16[16,1024,128]{2,1,0:T(8,128)(2,1)}, s32[]{:T(128)}) %tuple.104), condition=%wide.while_cond.1, body=%wide.while_body.1.sunk | while | flops 2 | bytes 525401 | solution.py:58
  76.1 2.5 bitcast_dynamic-update-slice_fusion.11
  116.2 8.0 %select_select_fusion = (bf16[16,1024,128]{2,1,0:T(8,128)(2,1)}, bf16[16,1024,128]{2,1,0:T(8,128)(2,1)}) fusion(bf16[16,1024,128]{2,1,0:T(8,128)(2,1)} %get-tuple-element.128, pred[16,1024]{1,0:T(8,128)(4,1)S(1)} %get-tuple-element.196, pred[]{:T(512)S(6)} %eq.7, bf16[16,1024,128]{2,1,0:T(8,128)(2,1)} %get-tuple-element.120, ...), kind=kLoop, calls=%fused_computation.23 | loop fusion | flops 8388608 | bytes 16809986 | tf_op jit(solution)/shard_map/jit(_where)/select_n | solution.py:19
  129.5 9.5 %collective-permute-done = bf16[1024,128]{1,0:T(8,128)(2,1)S(1)} collective-permute-done((bf16[1024,128]{1,0:T(8,128)(2,1)S(1)}, bf16[1024,128]{1,0:T(8,128)(2,1)S(1)}, u32[]{:S(2)}, u32[]{:S(2)}) %collective-permute-start) | collective-permute-done | bytes 262176 | tf_op jit(solution)/shard_map/ppermute | solution.py:15
  141.0 4.7 reduce-window.16
  148.1 4.5 reduce-window.14
  154.0 233.3 %all-reduce.17.cloned.1.call-done = (bf16[16,1024,128]{2,1,0:T(8,128)(2,1)}, bf16[16,1024,128]{2,1,0:T(8,128)(2,1)}) async-done(((bf16[16,1024,128]{2,1,0:T(8,128)(2,1)}, bf16[16,1024,128]{2,1,0:T(8,128)(2,1)}), (bf16[16,1024,128]{2,1,0:T(8,128)(2,1)}, bf16[16,1024,128]{2,1,0:T(8,128)(2,1)})) %all-reduce.17.cloned.1.call-update) | async-done | bytes 8388624 | tf_op jit(solution)/shard_map/psum | solution.py:20
  387.3 3.2 multiply_reduce_fusion
  390.4 143.4 %while.26 = (s32[]{:T(128)}, f32[4,4,1024]{2,1,0:T(4,128)S(1)}, bf16[4,4,1024,128]{3,2,1,0:T(8,128)(2,1)}, bf16[1024,1152]{1,0:T(8,128)(2,1)S(1)}, s32[]{:T(128)}, /*index=5*/f32[]{:T(128)}) while((s32[]{:T(128)}, f32[4,4,1024]{2,1,0:T(4,128)S(1)}, bf16[4,4,1024,128]{3,2,1,0:T(8,128)(2,1)}, bf16[1024,1152]{1,0:T(8,128)(2,1)S(1)}, s32[]{:T(128)}, ...), condition=%wide.region_3.4_spmd, body=%wide.region_1.3_spmd.sunk | while | flops 1208544768 | bytes 29483620 | solution.py:45
  390.5 4.3 fusion.23
  394.7 19.8 %rev.28 = f32[4,128,1152]{2,1,0:T(8,128)} reverse(f32[4,128,1152]{2,1,0:T(8,128)} %fusion.23), dimensions={2} | reverse | bytes 4718592 | tf_op jit(solution)/shard_map/while/body/eval_jaxpr/rev | solution.py:25
  414.5 3.5 pad.40
  418.0 5.8 reshape.322
  426.3 4.3 fusion.23
  430.6 19.8 %rev.28 = f32[4,128,1152]{2,1,0:T(8,128)} reverse(f32[4,128,1152]{2,1,0:T(8,128)} %fusion.23), dimensions={2} | reverse | bytes 4718592 | tf_op jit(solution)/shard_map/while/body/eval_jaxpr/rev | solution.py:25
  450.3 3.5 pad.40
  453.8 5.8 reshape.322
  462.2 4.3 fusion.23
  466.4 19.8 %rev.28 = f32[4,128,1152]{2,1,0:T(8,128)} reverse(f32[4,128,1152]{2,1,0:T(8,128)} %fusion.23), dimensions={2} | reverse | bytes 4718592 | tf_op jit(solution)/shard_map/while/body/eval_jaxpr/rev | solution.py:25
  486.2 3.5 pad.40
  489.6 5.8 reshape.322
  498.0 4.3 fusion.23
  502.3 19.8 %rev.28 = f32[4,128,1152]{2,1,0:T(8,128)} reverse(f32[4,128,1152]{2,1,0:T(8,128)} %fusion.23), dimensions={2} | reverse | bytes 4718592 | tf_op jit(solution)/shard_map/while/body/eval_jaxpr/rev | solution.py:25
  522.0 3.5 pad.40
  525.5 5.8 reshape.322
  534.5 143.4 %while.27 = (s32[]{:T(128)}, f32[4,4,1024]{2,1,0:T(4,128)S(1)}, bf16[4,4,1024,128]{3,2,1,0:T(8,128)(2,1)}, bf16[1024,1152]{1,0:T(8,128)(2,1)S(1)}, s32[]{:T(128)}, /*index=5*/f32[]{:T(128)}) while((s32[]{:T(128)}, f32[4,4,1024]{2,1,0:T(4,128)S(1)}, bf16[4,4,1024,128]{3,2,1,0:T(8,128)(2,1)}, bf16[1024,1152]{1,0:T(8,128)(2,1)S(1)}, ...), condition=%wide.region_15.16_spmd, body=%wide.region_13.15_spmd.sunk | while | flops 1208544768 | bytes 29483620 | solution.py:45
  534.5 4.3 fusion.26
  538.8 19.8 %rev.30 = f32[4,128,1152]{2,1,0:T(8,128)} reverse(f32[4,128,1152]{2,1,0:T(8,128)} %fusion.26), dimensions={2} | reverse | bytes 4718592 | tf_op jit(solution)/shard_map/while/body/eval_jaxpr/rev | solution.py:25
  558.6 3.5 pad.41
  562.0 5.8 reshape.323
  570.4 4.3 fusion.26
  574.6 19.8 %rev.30 = f32[4,128,1152]{2,1,0:T(8,128)} reverse(f32[4,128,1152]{2,1,0:T(8,128)} %fusion.26), dimensions={2} | reverse | bytes 4718592 | tf_op jit(solution)/shard_map/while/body/eval_jaxpr/rev | solution.py:25
  594.4 3.5 pad.41
  597.9 5.8 reshape.323
  606.2 4.3 fusion.26
  610.5 19.8 %rev.30 = f32[4,128,1152]{2,1,0:T(8,128)} reverse(f32[4,128,1152]{2,1,0:T(8,128)} %fusion.26), dimensions={2} | reverse | bytes 4718592 | tf_op jit(solution)/shard_map/while/body/eval_jaxpr/rev | solution.py:25
  630.2 3.5 pad.41
  633.7 5.8 reshape.323
  642.1 4.3 fusion.26
  646.3 19.8 %rev.30 = f32[4,128,1152]{2,1,0:T(8,128)} reverse(f32[4,128,1152]{2,1,0:T(8,128)} %fusion.26), dimensions={2} | reverse | bytes 4718592 | tf_op jit(solution)/shard_map/while/body/eval_jaxpr/rev | solution.py:25
  666.1 3.5 pad.41
  669.6 5.8 reshape.323
  678.6 3.2 multiply_reduce_fusion.1
  684.2 11.9 %all-reduce.15.cloned.1.call-done = (f32[16,1024]{1,0:T(8,128)}, f32[16,1024]{1,0:T(8,128)}, f32[16,1024]{1,0:T(8,128)}, f32[16,1024]{1,0:T(8,128)}) async-done(((f32[16,1024]{1,0:T(8,128)}, f32[16,1024]{1,0:T(8,128)}, f32[16,1024]{1,0:T(8,128)}, f32[16,1024]{1,0:T(8,128)}), (f32[16,1024]{1,0:T(8,128)}, f32[16,1024]{1,0:T(8,128)}, f32[16,1024]{1,0:T(8,128)}, ...) | async-done | bytes 262160 | tf_op jit(solution)/shard_map/psum | solution.py:84
  698.8 42.0 %all-reduce.8 = (f32[256]{0:T(256)S(1)}, f32[256]{0:T(256)S(1)}) all-reduce(f32[256]{0:T(256)S(1)} %dynamic-update-slice.5, f32[256]{0:T(256)S(1)} %dynamic-update-slice.4), channel_id=3, replica_groups=mesh['tm'=16,'sec'=2] {'tm'}, use_global_device_ids=true, to_apply=%add.7 | all-reduce | flops 512 | bytes 4096
  (194 shorter events, 140.2 us)
Async XLA Ops:
  6.5 380.7 %all-reduce.17.cloned.1.call-start = ((), (), s32[]{:S(2)}) async-start(), calls=%async_computation.1 | async-start | bytes 16777216 | tf_op jit(solution)/shard_map/psum | solution.py:20
  124.2 2.4 copy-start
  124.2 571.9 %all-reduce.15.cloned.1.call-start = ((), (), s32[]{:S(2)}) async-start(), calls=%async_computation | async-start | bytes 524288 | tf_op jit(solution)/shard_map/psum | solution.py:84
  125.3 13.7 %collective-permute-start = (bf16[1024,128]{1,0:T(8,128)(2,1)S(1)}, bf16[1024,128]{1,0:T(8,128)(2,1)S(1)}, u32[]{:S(2)}, u32[]{:S(2)}) collective-permute-start(bf16[1024,128]{1,0:T(8,128)(2,1)S(1)} %slice.81), channel_id=1, source_target_pairs={{2,0},{4,2},{6,4},{8,6},{10,8},{12,10},{14,12},{16,14},{18,16},{20... | collective-permute-start | bytes 786440 | tf_op jit(solution)/shard_map/ppermute | solution.py:15
  423.8 1.7 slice-start
  459.6 1.7 slice-start
  495.4 1.7 slice-start
  531.3 1.7 slice-start
  567.8 1.7 slice-start.1
  603.7 1.7 slice-start.1
  639.5 1.7 slice-start.1
  675.4 1.7 slice-start.1
Sparse Core Ops, SparseCore 0:
  124.4 262.8 all-reduce.16
  678.7 17.4 all-reduce.14
